TPU v7x, 512 devices: a whole 4x8x8 slice. The times are simulated.
512 devices in a mesh: expert: 64 (over x, z, core), group: 8 (over y).
Axes of the slice: x: 4, y: 8, z: 8, core: 2. Of those that a mesh axis runs over, the one named last changes fastest.
Arguments:
- tokens: bfloat16 [4096, 4096], P('expert', 'group'), may hold values from -6 to 6
- gate_weight: bfloat16 [64, 1536, 4096], P('expert', 'group'), may hold values from -0.09375 to 0.09375
- up_weight: bfloat16 [64, 1536, 4096], P('expert', 'group'), may hold values from -0.09375 to 0.09375
- down_weight: bfloat16 [64, 1536, 4096], P('expert', 'group'), may hold values from -0.15625 to 0.15625
- expert_ids: int32 [4096, 8], P('expert'), may hold values from 0 to 63, all different within a row; in each aligned block of 64 rows (0 to 63, 64 to 127, ...) at most 12 rows name the same one
- gate_scores: bfloat16 [4096, 8], P('expert'), may hold values from 0.19921875 to 1
Outputs:
- mixed: bfloat16 [4096, 4096], P('expert', 'group')
Inputs may be any that keep to these rules, and one draw needn't show every extreme that they name: `expert_ids`: the 8 experts of a token are distinct; within the 64 rows of one device no expert is named by more than 12 rows, a bound that some block reaches.
All inputs are finite; a program needn't handle non-finite values.
Results may differ from a plain program's by a relative error of at most 0.019.
Values may be sent and summed in bfloat16 or wider, within the bound.
No kernel may reach another device: no remote copies, remote signals or barrier semaphores. Data moves between devices by JAX's collectives and lax.ppermute only.
A program may use at most 128 MiB of HBM per device.

v0:
```python
import jax
import jax.numpy as jnp
from jax import lax
from jax.sharding import PartitionSpec as P


def per_device(tokens, gate_weight, up_weight, down_weight, expert_ids, gate_scores):
    experts = lax.axis_size("expert")
    tok_rows = tokens.shape[0]
    top_count = expert_ids.shape[1]
    capacity = tok_rows * top_count * 3 // (2 * experts)
    flat_ids = expert_ids.reshape(-1)
    onehot = (flat_ids[:, None] == jnp.arange(experts, dtype=jnp.int32)[None, :]).astype(jnp.int32)
    before = jnp.cumsum(onehot, axis=0) - onehot
    slot_index = jnp.sum(before * onehot, axis=1).reshape(tok_rows, top_count)
    slot_keys = expert_ids * capacity + slot_index
    columns = jnp.arange(experts * capacity, dtype=jnp.int32)
    matches = slot_keys[:, :, None] == columns[None, None, :]
    selector = jnp.any(matches, axis=1).astype(jnp.bfloat16)
    weights = jnp.sum(
        jnp.where(matches, gate_scores[:, :, None].astype(jnp.float32), 0.0), axis=1
    ).astype(jnp.bfloat16)
    whole_rows = lax.all_gather(tokens, "group", axis=1, tiled=True)
    placed = lax.dot_general(
        selector, whole_rows, (((0,), (0,)), ((), ())), preferred_element_type=jnp.float32
    )
    arrived = lax.all_to_all(
        placed.astype(jnp.bfloat16).reshape(experts, capacity, whole_rows.shape[1]),
        "expert",
        split_axis=0,
        concat_axis=0,
        tiled=True,
    )
    row_block = arrived.reshape(-1, arrived.shape[2])
    gate_value = lax.dot_general(
        row_block, gate_weight[0], (((1,), (1,)), ((), ())), preferred_element_type=jnp.float32
    )
    up_value = lax.dot_general(
        row_block, up_weight[0], (((1,), (1,)), ((), ())), preferred_element_type=jnp.float32
    )
    hidden = (jax.nn.silu(gate_value) * up_value).astype(jnp.bfloat16)
    partial_value = jnp.dot(hidden, down_weight[0], preferred_element_type=jnp.float32)
    returned = lax.all_to_all(
        partial_value.astype(jnp.bfloat16).reshape(arrived.shape),
        "expert",
        split_axis=0,
        concat_axis=0,
        tiled=True,
    )
    combined = jnp.dot(
        weights, returned.reshape(experts * capacity, -1), preferred_element_type=jnp.float32
    )
    return lax.psum_scatter(combined.astype(jnp.bfloat16), "group", scatter_dimension=1, tiled=True)


def solution(mesh):
    placed = (
        P("expert", "group"),
        P("expert", "group", None),
        P("expert", "group", None),
        P("expert", "group", None),
        P("expert", None),
        P("expert", None),
    )
    return jax.shard_map(
        per_device, mesh=mesh, in_specs=placed, out_specs=P("expert", "group"), check_vma=False
    )
```

profile of v0, /device:TPU:2, one launch (start us, length us, event | category | flops | bytes accessed | tf_op | source)
XLA Modules:
  0.0 540.2 jit_solution(18164312794375199998)
XLA Ops:
  6.5 0.9 copy.21
  7.4 0.1 eq.42
  7.5 0.1 eq.38
  7.6 1.2 reduce-window.6
  8.8 0.2 slice_reduce_fusion
  9.1 0.1 fusion.22
  9.2 0.1 reshape.36
  9.4 0.7 multiply_add_fusion
  10.2 0.5 fusion.5
  10.7 27.1 %all_gather.3 = bf16[64,4096]{1,0:T(8,128)(2,1)S(1)} all-gather(bf16[64,512]{1,0:T(8,128)(2,1)} %param.6), channel_id=1, replica_groups=mesh['expert'=64,'group'=8] {'group'}, dimensions={1}, use_global_device_ids=true | all-gather | bytes 589824 | tf_op jit(solution)/shard_map/all_gather | solution.py:23
  37.9 4.6 convolution_convert_fusion
  42.4 9.8 %reshape.37 = bf16[64,12,4096]{2,1,0:T(8,128)(2,1)} reshape(bf16[768,4096]{1,0:T(8,128)(2,1)} %convolution_convert_fusion) | data formatting | bytes 12582912 | tf_op jit(solution)/shard_map/reshape | solution.py:28
  52.2 198.1 %all_to_all.10 = bf16[64,12,4096]{2,1,0:T(8,128)(2,1)} all-to-all(bf16[64,12,4096]{2,1,0:T(8,128)(2,1)} %reshape.37), channel_id=1, replica_groups=mesh['expert'=64,'group'=8] {'expert'}, dimensions={0} | all-to-all | bytes 12582912 | tf_op jit(solution)/shard_map/all_to_all | solution.py:27
  250.3 10.1 %reshape.38 = bf16[768,4096]{1,0:T(8,128)(2,1)} reshape(bf16[64,12,4096]{2,1,0:T(8,128)(2,1)} %all_to_all.10) | data formatting | bytes 12582912 | tf_op jit(solution)/shard_map/reshape | solution.py:34
  260.4 5.8 %fusion.3 = f32[768,192]{0,1:T(8,128)} fusion(bf16[768,4096]{1,0:T(8,128)(2,1)} %reshape.38, bf16[1,192,4096]{2,1,0:T(8,128)(2,1)S(1)} %copy-done.2), kind=kOutput, calls=%fused_computation.6 | convolution fusion | flops 1207959552 | bytes 8454144 | tf_op jit(solution)/shard_map/dot_general | solution.py:35
  266.3 13.5 %convolution_convert_fusion.1 = bf16[768,4096]{1,0:T(8,128)(2,1)} fusion(bf16[1,192,4096]{2,1,0:T(8,128)(2,1)S(1)} %copy-done, bf16[768,4096]{1,0:T(8,128)(2,1)} %reshape.38, bf16[1,192,4096]{2,1,0:T(8,128)(2,1)} %param.8, f32[768,192]{0,1:T(8,128)} %fusion.3), kind=kOutput, calls=%fused_computation.1 | convolution fusion | flops 2419949568 | bytes 16318464 | tf_op jit(solution)/shard_map/dot_general | solution.py:42
  279.7 9.8 %reshape.39 = bf16[64,12,4096]{2,1,0:T(8,128)(2,1)} reshape(bf16[768,4096]{1,0:T(8,128)(2,1)} %convolution_convert_fusion.1) | data formatting | bytes 12582912 | tf_op jit(solution)/shard_map/reshape | solution.py:44
  289.5 8.0 %all-to-all-start.1 = ((bf16[64,12,4096]{2,1,0:T(8,128)(2,1)}), bf16[64,12,4096]{2,1,0:T(8,128)(2,1)}, u32[]{:S(2)}, u32[]{:S(2)}) async-start(bf16[64,12,4096]{2,1,0:T(8,128)(2,1)} %reshape.39), calls=%async_computation.1 | async-start | bytes 16777216 | tf_op jit(solution)/shard_map/all_to_all | solution.py:43
  297.6 0.1 copy.26
  297.7 0.6 select_reduce_fusion
  298.3 183.5 %all-to-all-done.1 = bf16[64,12,4096]{2,1,0:T(8,128)(2,1)} async-done(((bf16[64,12,4096]{2,1,0:T(8,128)(2,1)}), bf16[64,12,4096]{2,1,0:T(8,128)(2,1)}, u32[]{:S(2)}, u32[]{:S(2)}) %all-to-all-start.1) | async-done | bytes 6291488 | tf_op jit(solution)/shard_map/all_to_all | solution.py:43
  481.8 9.9 %reshape.40 = bf16[768,4096]{1,0:T(8,128)(2,1)} reshape(bf16[64,12,4096]{2,1,0:T(8,128)(2,1)} %all-to-all-done.1) | data formatting | bytes 12582912 | tf_op jit(solution)/shard_map/reshape | solution.py:51
  491.6 4.8 convolution_convert_fusion.2
  496.5 36.9 %reduce-scatter.2.cloned.1.call-done = bf16[64,512]{1,0:T(8,128)(2,1)} async-done(((bf16[64,4096]{1,0:T(8,128)(2,1)}), bf16[64,512]{1,0:T(8,128)(2,1)}) %reduce-scatter.2.cloned.1.call-update) | async-done | bytes 65552 | tf_op jit(solution)/shard_map/reduce_scatter | solution.py:53
  (13 shorter events, 0.3 us)
Async XLA Ops:
  6.5 259.7 %copy-start = (bf16[1,192,4096]{2,1,0:T(8,128)(2,1)S(1)}, bf16[1,192,4096]{2,1,0:T(8,128)(2,1)}, u32[]{:S(2)}) copy-start(bf16[1,192,4096]{2,1,0:T(8,128)(2,1)} %param.9) | copy-start | bytes 4718596
  250.3 10.1 %copy-start.2 = (bf16[1,192,4096]{2,1,0:T(8,128)(2,1)S(1)}, bf16[1,192,4096]{2,1,0:T(8,128)(2,1)}, u32[]{:S(2)}) copy-start(bf16[1,192,4096]{2,1,0:T(8,128)(2,1)} %param.7) | copy-start | bytes 4718596
  289.5 8.1 %copy-start.1 = (bf16[64,8]{0,1:T(8,128)(2,1)S(1)}, bf16[64,8]{0,1:T(8,128)(2,1)}, u32[]{:S(2)}) copy-start(bf16[64,8]{0,1:T(8,128)(2,1)} %param.11) | copy-start | bytes 3076
  289.5 192.3 %all-to-all-start.1 = ((bf16[64,12,4096]{2,1,0:T(8,128)(2,1)}), bf16[64,12,4096]{2,1,0:T(8,128)(2,1)}, u32[]{:S(2)}, u32[]{:S(2)}) async-start(bf16[64,12,4096]{2,1,0:T(8,128)(2,1)} %reshape.39), calls=%async_computation.1 | async-start | bytes 16777216 | tf_op jit(solution)/shard_map/all_to_all | solution.py:43
  297.6 235.8 %reduce-scatter.2.cloned.1.call-start = ((), (), s32[]{:S(2)}) async-start(), calls=%async_computation.3 | async-start | bytes 589824 | tf_op jit(solution)/shard_map/reduce_scatter | solution.py:53
Sparse Core Ops, SparseCore 0:
  496.6 36.7 reduce-scatter.1
where the time goes:
time: 541 us; the launch traced here: 540 us
  blocking collectives  225 us (42%)
  waiting for transfers between devices  220 us (41%)
  local copies, waits for them, and re-layouts  41.1 us (8%)
  matrix products  28.6 us (5%)
  between operations  13.5 us (2%)
  starting transfers between devices  8.08 us (1%)
    all_to_all x1, blocking collectives, per_device(): lax.all_to_all(placed.astype(jnp.bfloat16).reshape(experts, capacity, who...  198 us
    all_to_all x1, waiting for transfers between devices, per_device(): lax.all_to_all(partial_value.astype(jnp.bfloat16).reshape(arrived.shape),...  184 us
    reduce_scatter x1, waiting for transfers between devices, per_device(): lax.psum_scatter(combined.astype(jnp.bfloat16), 'group', scatter_dimensio...  36.9 us
    all_gather x1, blocking collectives, per_device(): whole_rows = lax.all_gather(tokens, 'group', axis=1, tiled=True)  27.1 us
    dot_general x1, matrix products, per_device(): jnp.dot(hidden, down_weight[0], preferred_element_type=jnp.float32)  13.5 us
  transfers between devices with their start and end apart: 2, of which 2 were waited for; matrix products, arithmetic and copies ran while one was open for 0% of the time, Pallas kernels for 0%

commit v1 on v0

--- a/solution.py
+++ b/solution.py
@@ -2,6 +2,13 @@
 import jax.numpy as jnp
 from jax import lax
 from jax.sharding import PartitionSpec as P
+
+
+def exchange_gather(value, axis, dim):
+    peers = lax.axis_size(axis)
+    pieces = jnp.stack([value for _ in range(peers)])
+    pieces = lax.all_to_all(pieces, axis, split_axis=0, concat_axis=0)
+    return jnp.concatenate(pieces, axis=dim)
 
 
 def per_device(tokens, gate_weight, up_weight, down_weight, expert_ids, gate_scores):
@@ -20,7 +27,7 @@
     weights = jnp.sum(
         jnp.where(matches, gate_scores[:, :, None].astype(jnp.float32), 0.0), axis=1
     ).astype(jnp.bfloat16)
-    whole_rows = lax.all_gather(tokens, "group", axis=1, tiled=True)
+    whole_rows = exchange_gather(tokens, "group", 1)
     placed = lax.dot_general(
         selector, whole_rows, (((0,), (0,)), ((), ())), preferred_element_type=jnp.float32
     )

time: 541 us -> 532 us (0.983)
  blocking collectives: 225 us -> 198 us
  waiting for transfers between devices: 220 us -> 230 us
  starting transfers between devices: 8.08 us -> 15.2 us
    all_gather x1 -> x0, blocking collectives: 27.1 us -> none  [per_device(): whole_rows = lax.all_gather(tokens, 'group', axis=1, tiled=True)]
    all_to_all x0 -> x1, waiting for transfers between devices: none -> 13.4 us  [exchange_gather(): pieces = lax.all_to_all(pieces, axis, split_axis=0, concat_axis=0)]
    all_to_all x0 -> x1, starting transfers between devices: none -> 7.1 us  [exchange_gather(): pieces = lax.all_to_all(pieces, axis, split_axis=0, concat_axis=0)]
  transfers between devices with their start and end apart: 2 -> 3, of which waited for: 2 -> 3; matrix products, arithmetic and copies ran while one was open for 0% -> 1% of each run, Pallas kernels for 0% -> 0%
where the time goes in v1:
time: 532 us; the launch traced here: 531 us
  waiting for transfers between devices  230 us (43%)
  blocking collectives  198 us (37%)
  local copies, waits for them, and re-layouts  42.7 us (8%)
  matrix products  28 us (5%)
  starting transfers between devices  15.2 us (3%)
  between operations  13.5 us (3%)
    all_to_all x1, blocking collectives, per_device(): lax.all_to_all(placed.astype(jnp.bfloat16).reshape(experts, capacity, who...  198 us
    all_to_all x1, waiting for transfers between devices, per_device(): lax.all_to_all(partial_value.astype(jnp.bfloat16).reshape(arrived.shape),...  184 us
    reduce_scatter x1, waiting for transfers between devices, per_device(): lax.psum_scatter(combined.astype(jnp.bfloat16), 'group', scatter_dimensio...  33 us
    all_to_all x1, waiting for transfers between devices, exchange_gather(): pieces = lax.all_to_all(pieces, axis, split_axis=0, concat_axis=0)  13.4 us
    dot_general x1, matrix products, per_device(): jnp.dot(hidden, down_weight[0], preferred_element_type=jnp.float32)  13.3 us
  transfers between devices with their start and end apart: 3, of which 3 were waited for; matrix products, arithmetic and copies ran while one was open for 1% of the time, Pallas kernels for 0%

profile of v1, /device:TPU:2, one launch (start us, length us, event | category | flops | bytes accessed | tf_op | source)
XLA Modules:
  0.0 530.7 jit_solution(7177577532529289477)
XLA Ops:
  6.5 1.8 stack.2
  8.3 7.1 %all-to-all-start = ((bf16[8,64,512]{2,1,0:T(8,128)(2,1)}), bf16[8,64,512]{2,1,0:T(8,128)(2,1)S(1)}, u32[]{:S(2)}, u32[]{:S(2)}) async-start(bf16[8,64,512]{2,1,0:T(8,128)(2,1)} %stack.2), calls=%async_computation | async-start | bytes 1048576 | tf_op jit(solution)/shard_map/all_to_all | solution.py:10
  15.4 0.8 copy.29
  16.2 0.1 eq.42
  16.4 1.2 reduce-window.6
  17.6 0.2 slice_reduce_fusion
  17.9 0.1 fusion.22
  18.2 0.7 multiply_add_fusion
  19.0 0.5 fusion.5
  19.5 13.4 %all-to-all-done = bf16[8,64,512]{2,1,0:T(8,128)(2,1)S(1)} async-done(((bf16[8,64,512]{2,1,0:T(8,128)(2,1)}), bf16[8,64,512]{2,1,0:T(8,128)(2,1)S(1)}, u32[]{:S(2)}, u32[]{:S(2)}) %all-to-all-start) | async-done | bytes 524320 | tf_op jit(solution)/shard_map/all_to_all | solution.py:10
  33.0 4.6 convolution_convert_fusion
  37.5 9.8 %reshape.47 = bf16[64,12,4096]{2,1,0:T(8,128)(2,1)} reshape(bf16[768,4096]{1,0:T(8,128)(2,1)} %convolution_convert_fusion) | data formatting | bytes 12582912 | tf_op jit(solution)/shard_map/reshape | solution.py:35
  47.3 198.1 %all_to_all.15 = bf16[64,12,4096]{2,1,0:T(8,128)(2,1)} all-to-all(bf16[64,12,4096]{2,1,0:T(8,128)(2,1)} %reshape.47), channel_id=1, replica_groups=mesh['expert'=64,'group'=8] {'expert'}, dimensions={0} | all-to-all | bytes 12582912 | tf_op jit(solution)/shard_map/all_to_all | solution.py:34
  245.4 10.0 %reshape.48 = bf16[768,4096]{1,0:T(8,128)(2,1)} reshape(bf16[64,12,4096]{2,1,0:T(8,128)(2,1)} %all_to_all.15) | data formatting | bytes 12582912 | tf_op jit(solution)/shard_map/reshape | solution.py:41
  255.4 5.4 %fusion.3 = f32[768,192]{0,1:T(8,128)S(1)} fusion(bf16[768,4096]{1,0:T(8,128)(2,1)} %reshape.48, bf16[1,192,4096]{2,1,0:T(8,128)(2,1)} %param.7), kind=kOutput, calls=%fused_computation.6 | convolution fusion | flops 1207959552 | bytes 8454144 | tf_op jit(solution)/shard_map/dot_general | solution.py:42
  260.8 13.3 %convolution_convert_fusion.1 = bf16[768,4096]{1,0:T(8,128)(2,1)} fusion(bf16[1,192,4096]{2,1,0:T(8,128)(2,1)S(1)} %copy-done, bf16[768,4096]{1,0:T(8,128)(2,1)} %reshape.48, bf16[1,192,4096]{2,1,0:T(8,128)(2,1)} %param.8, f32[768,192]{0,1:T(8,128)S(1)} %fusion.3), kind=kOutput, calls=%fused_computation.1 | convolution fusion | flops 2419949568 | bytes 16318464 | tf_op jit(solution)/shard_map/dot_general | solution.py:49
  274.1 9.7 %reshape.49 = bf16[64,12,4096]{2,1,0:T(8,128)(2,1)} reshape(bf16[768,4096]{1,0:T(8,128)(2,1)} %convolution_convert_fusion.1) | data formatting | bytes 12582912 | tf_op jit(solution)/shard_map/reshape | solution.py:51
  283.9 8.1 %all-to-all-start.2 = ((bf16[64,12,4096]{2,1,0:T(8,128)(2,1)}), bf16[64,12,4096]{2,1,0:T(8,128)(2,1)}, u32[]{:S(2)}, u32[]{:S(2)}) async-start(bf16[64,12,4096]{2,1,0:T(8,128)(2,1)} %reshape.49), calls=%async_computation.2 | async-start | bytes 16777216 | tf_op jit(solution)/shard_map/all_to_all | solution.py:50
  292.0 0.1 copy.34
  292.1 0.6 select_reduce_fusion
  292.6 183.5 %all-to-all-done.2 = bf16[64,12,4096]{2,1,0:T(8,128)(2,1)} async-done(((bf16[64,12,4096]{2,1,0:T(8,128)(2,1)}), bf16[64,12,4096]{2,1,0:T(8,128)(2,1)}, u32[]{:S(2)}, u32[]{:S(2)}) %all-to-all-start.2) | async-done | bytes 6291488 | tf_op jit(solution)/shard_map/all_to_all | solution.py:50
  476.2 9.9 %reshape.50 = bf16[768,4096]{1,0:T(8,128)(2,1)} reshape(bf16[64,12,4096]{2,1,0:T(8,128)(2,1)} %all-to-all-done.2) | data formatting | bytes 12582912 | tf_op jit(solution)/shard_map/reshape | solution.py:58
  486.0 4.8 convolution_convert_fusion.2
  490.8 33.0 %reduce-scatter.2.cloned.1.call-done = bf16[64,512]{1,0:T(8,128)(2,1)} async-done(((bf16[64,4096]{1,0:T(8,128)(2,1)}), bf16[64,512]{1,0:T(8,128)(2,1)}) %reduce-scatter.2.cloned.1.call-update) | async-done | bytes 65552 | tf_op jit(solution)/shard_map/reduce_scatter | solution.py:60
  (14 shorter events, 0.5 us)
Async XLA Ops:
  6.5 254.3 %copy-start = (bf16[1,192,4096]{2,1,0:T(8,128)(2,1)S(1)}, bf16[1,192,4096]{2,1,0:T(8,128)(2,1)}, u32[]{:S(2)}) copy-start(bf16[1,192,4096]{2,1,0:T(8,128)(2,1)} %param.9) | copy-start | bytes 4718596
  8.3 24.6 %all-to-all-start = ((bf16[8,64,512]{2,1,0:T(8,128)(2,1)}), bf16[8,64,512]{2,1,0:T(8,128)(2,1)S(1)}, u32[]{:S(2)}, u32[]{:S(2)}) async-start(bf16[8,64,512]{2,1,0:T(8,128)(2,1)} %stack.2), calls=%async_computation | async-start | bytes 1048576 | tf_op jit(solution)/shard_map/all_to_all | solution.py:10
  283.8 8.1 %copy-start.1 = (bf16[64,8]{0,1:T(8,128)(2,1)S(1)}, bf16[64,8]{0,1:T(8,128)(2,1)}, u32[]{:S(2)}) copy-start(bf16[64,8]{0,1:T(8,128)(2,1)} %param.11) | copy-start | bytes 3076
  283.9 192.3 %all-to-all-start.2 = ((bf16[64,12,4096]{2,1,0:T(8,128)(2,1)}), bf16[64,12,4096]{2,1,0:T(8,128)(2,1)}, u32[]{:S(2)}, u32[]{:S(2)}) async-start(bf16[64,12,4096]{2,1,0:T(8,128)(2,1)} %reshape.49), calls=%async_computation.2 | async-start | bytes 16777216 | tf_op jit(solution)/shard_map/all_to_all | solution.py:50
  291.9 231.9 %reduce-scatter.2.cloned.1.call-start = ((), (), s32[]{:S(2)}) async-start(), calls=%async_computation.4 | async-start | bytes 589824 | tf_op jit(solution)/shard_map/reduce_scatter | solution.py:60
Sparse Core Ops, SparseCore 0:
  490.9 32.8 reduce-scatter.1
